TPU v7x, 32 devices: a whole 2x2x4 slice. The times are simulated.
32 devices in a mesh: req: 8 (over z, y), tp: 4 (over x, core).
Axes of the slice: x: 2, y: 2, z: 4, core: 2. Of those that a mesh axis runs over, the one named last changes fastest.
Arguments:
- tokens_in: bfloat16 [24, 4, 2048], P('req'), may hold values from -6 to 6
- attn_norm: bfloat16 [2048], replicated, may hold values from 0.099609375 to 1.8984375
- qkv_weight: bfloat16 [2048, 3, 2048], P(None, None, 'tp'), may hold values from -0.125 to 0.125
- qkv_bias: bfloat16 [3, 2048], P(None, 'tp'), may hold values from -12 to 12
- out_weight: bfloat16 [2048, 2048], P('tp'), may hold values from -0.125 to 0.125
- cache_keys: bfloat16 [320, 128, 2048], P('req', None, 'tp'), may hold values from -12 to 12
- cache_values: bfloat16 [320, 128, 2048], P('req', None, 'tp'), may hold values from -6 to 6
- page_table: int32 [24, 37], replicated, may hold values from -1 to 319, as said below
- cache_lengths: int32 [24], replicated, may hold values from 1 to 4736, as said below
- mlp_norm: bfloat16 [2048], replicated, may hold values from 0.099609375 to 1.8984375
- routes: int32 [24, 4, 4], P('req'), may hold values from 0 to 7, all different within a row; in each aligned block of 12 rows (0 to 11, 12 to 23, ..., all dimensions but the last counted through in order) at most 6 rows name the same one
- route_gates: float32 [24, 4, 4], P('req'), may hold values from 0.05 to 0.5
- expert_w_gate: bfloat16 [8, 2048, 1408], P('req', None, 'tp'), may hold values from -0.125 to 0.125
- expert_w_up: bfloat16 [8, 2048, 1408], P('req', None, 'tp'), may hold values from -0.125 to 0.125
- expert_w_down: bfloat16 [8, 1408, 2048], P('req', 'tp'), may hold values from -0.15625 to 0.15625
- shared_w_gate: bfloat16 [2048, 5632], P('tp', 'req'), may hold values from -0.125 to 0.125
- shared_w_up: bfloat16 [2048, 5632], P('tp', 'req'), may hold values from -0.125 to 0.125
- shared_w_down: bfloat16 [5632, 2048], P('req', 'tp'), may hold values from -0.078125 to 0.078125
- shared_switch: bfloat16 [2048], replicated, may hold values from -0.125 to 0.125
Outputs:
- layer_out: bfloat16 [24, 4, 2048], P('req', None, 'tp')
Inputs may be any that keep to these rules, and one draw needn't show every extreme that they name: `page_table`: entry [r, j] is the pool page holding positions j*128 to (j+1)*128 - 1 of request r's cache, or -1. No pool page is named twice. 6 requests, drawn from the seed, have all 37 entries set, all outside the first 12 pages of every block of 40 pool pages; every other request r has exactly its first 4 entries set, all among pool pages (r // 3)*40 to (r // 3)*40 + 3*4 - 1. `cache_lengths`: A long request has 2368 to 4736 cached tokens, any other 1 to 512; both largest values occur in every draw. `routes`: the 4 experts of a token differ. Among the 12 tokens of each aligned block of rows (those of one index of req) no expert is named more than 6 times, and in some of those blocks one expert is named exactly 6 times.
All inputs are finite; a program needn't handle non-finite values.
Results may differ from a plain program's by a relative error of at most 0.006.
Values may be sent and summed in bfloat16 or wider, within the bound.
No kernel may reach another device: no remote copies, remote signals or barrier semaphores. Data moves between devices by JAX's collectives and lax.ppermute only.
A program may use at most 128 MiB of HBM per device.

v0:
```python
import math
import jax
import jax.numpy as jnp
from jax import lax
from jax.sharding import PartitionSpec as P

HD = 128
TOPK = 4
NEG = -1e30
EPS = 1e-06
THETA = 1000000.0
HIGHEST = lax.Precision.HIGHEST


def rms_norm(inputs, gain_vector):
    values = inputs.astype(jnp.float32)
    scaled = values * lax.rsqrt(jnp.mean(values * values, axis=-1, keepdims=True) + EPS)
    return (scaled * gain_vector.astype(jnp.float32)).astype(jnp.bfloat16)


def rotate(values, positions):
    half_dim = values.shape[-1] // 2
    exponents = jnp.arange(half_dim, dtype=jnp.float32) * (2.0 / values.shape[-1])
    frequency = jnp.power(THETA, -exponents)
    angles = positions.astype(jnp.float32)[..., None, None] * frequency
    cosines = jnp.cos(angles)
    sine_part = jnp.sin(angles)
    front_half = values[..., :half_dim]
    back_half = values[..., half_dim:]
    return jnp.concatenate(
        [
            front_half * cosines - back_half * sine_part,
            back_half * cosines + front_half * sine_part,
        ],
        axis=-1,
    )


def per_device(
    tokens_in,
    attn_norm,
    qkv_weight,
    qkv_bias,
    out_weight,
    cache_keys,
    cache_values,
    page_table,
    cache_lengths,
    mlp_norm,
    routes,
    route_gates,
    expert_w_gate,
    expert_w_up,
    expert_w_down,
    shared_w_gate,
    shared_w_up,
    shared_w_down,
    shared_switch,
):
    req_rows, step_count, model_width = tokens_in.shape
    head_width = qkv_weight.shape[2]
    local_heads = head_width // HD
    req_count = lax.axis_size("req")
    tp_count = lax.axis_size("tp")
    req_index = lax.axis_index("req")
    tp_index = lax.axis_index("tp")
    all_requests = page_table.shape[0]
    pool_here = cache_keys.shape[0]
    page_len = cache_keys.shape[1]
    score_scale = 1.0 / math.sqrt(HD)
    col_share = model_width // tp_count
    row_count = req_rows * step_count
    normed = rms_norm(tokens_in, attn_norm)
    projected = jnp.einsum(
        "rsd,dcf->rscf", normed, qkv_weight, preferred_element_type=jnp.float32
    ) + qkv_bias.astype(jnp.float32)
    own_lengths = lax.dynamic_slice_in_dim(cache_lengths, req_index * req_rows, req_rows)
    positions = own_lengths[:, None] + jnp.arange(step_count, dtype=jnp.int32)[None, :]
    head_shape = (req_rows, step_count, local_heads, HD)
    query_new = rotate(projected[:, :, 0].reshape(head_shape), positions).astype(jnp.bfloat16)
    key_new = rotate(projected[:, :, 1].reshape(head_shape), positions).astype(jnp.bfloat16)
    value_new = projected[:, :, 2].reshape(head_shape).astype(jnp.bfloat16)
    query_all = lax.all_gather(query_new, "req", axis=0, tiled=True)
    slot_ids = req_index * pool_here + jnp.arange(pool_here, dtype=jnp.int32)
    matches = (page_table[:, :, None] == slot_ids[None, None, :]).astype(jnp.int32)
    request_ids = jnp.arange(all_requests, dtype=jnp.int32)
    page_ids = jnp.arange(page_table.shape[1], dtype=jnp.int32)
    owner = jnp.sum(matches * request_ids[:, None, None], axis=(0, 1))
    logical = jnp.sum(matches * page_ids[None, :, None], axis=(0, 1))
    present = jnp.sum(matches, axis=(0, 1)) > 0
    token_pos = logical[:, None] * page_len + jnp.arange(page_len, dtype=jnp.int32)[None, :]
    live = present[:, None] & (token_pos < cache_lengths[owner][:, None])
    page_queries = query_all[owner]
    page_keys = cache_keys.reshape(pool_here, page_len, local_heads, HD)
    page_values = cache_values.reshape(pool_here, page_len, local_heads, HD)
    scores = (
        jnp.einsum("pshd,pkhd->pshk", page_queries, page_keys, preferred_element_type=jnp.float32)
        * score_scale
    )
    page_mask = live[:, None, None, :]
    masked = jnp.where(page_mask, scores, NEG)
    page_max = jnp.max(masked, axis=-1)
    weights = jnp.where(page_mask, jnp.exp(masked - page_max[..., None]), 0.0)
    page_sum = jnp.sum(weights, axis=-1)
    page_out = jnp.einsum(
        "pshk,pkhd->pshd",
        weights.astype(jnp.bfloat16),
        page_values,
        preferred_element_type=jnp.float32,
    )
    belongs = (owner[None, :] == request_ids[:, None]) & present[None, :]
    owned = belongs[:, :, None, None]
    local_max = jnp.max(jnp.where(owned, page_max[None], NEG), axis=1)
    factors = jnp.where(owned, jnp.exp(page_max[None] - local_max[:, None]), 0.0)
    local_out = jnp.einsum("rpsh,pshd->rshd", factors, page_out, precision=HIGHEST)
    local_sum = jnp.einsum("rpsh,psh->rsh", factors, page_sum, precision=HIGHEST)
    first_row = req_index * req_rows
    global_max = lax.pmax(local_max, "req")
    rescale = jnp.exp(local_max - global_max)
    summed_out, summed_sum = lax.psum((local_out * rescale[..., None], local_sum * rescale), "req")
    cache_max = lax.dynamic_slice_in_dim(global_max, first_row, req_rows)
    cache_out = lax.dynamic_slice_in_dim(summed_out, first_row, req_rows)
    cache_sum = lax.dynamic_slice_in_dim(summed_sum, first_row, req_rows)
    new_scores = (
        jnp.einsum("rshd,rthd->rsht", query_new, key_new, preferred_element_type=jnp.float32)
        * score_scale
    )
    causal = jnp.arange(step_count)[:, None] >= jnp.arange(step_count)[None, :]
    new_mask = causal[None, :, None, :]
    new_masked = jnp.where(new_mask, new_scores, NEG)
    new_max = jnp.max(new_masked, axis=-1)
    new_weights = jnp.where(new_mask, jnp.exp(new_masked - new_max[..., None]), 0.0)
    new_sum = jnp.sum(new_weights, axis=-1)
    new_out = jnp.einsum(
        "rsht,rthd->rshd",
        new_weights.astype(jnp.bfloat16),
        value_new,
        preferred_element_type=jnp.float32,
    )
    top_max = jnp.maximum(cache_max, new_max)
    cache_factor = jnp.exp(cache_max - top_max)
    new_factor = jnp.exp(new_max - top_max)
    attended = (cache_out * cache_factor[..., None] + new_out * new_factor[..., None]) / (
        cache_sum * cache_factor + new_sum * new_factor
    )[..., None]
    attended = attended.astype(jnp.bfloat16).reshape(row_count, head_width)
    attn_part = jnp.dot(attended, out_weight, preferred_element_type=jnp.float32)
    attn_full = lax.psum(attn_part, "tp")
    resid = tokens_in.reshape(row_count, model_width).astype(jnp.float32) + attn_full
    mixed = rms_norm(resid, mlp_norm)
    expert_count = req_count * expert_w_gate.shape[0]
    capacity = max(2, (row_count * TOPK + expert_count - 1) // expert_count)
    picks = routes.reshape(row_count * TOPK)
    gates_flat = route_gates.reshape(row_count * TOPK)
    expert_hot = (picks[:, None] == jnp.arange(expert_count, dtype=jnp.int32)[None, :]).astype(
        jnp.int32
    )
    slot_index = jnp.sum((jnp.cumsum(expert_hot, axis=0) - 1) * expert_hot, axis=1)
    destination = picks * capacity + slot_index
    dest_hot = (
        destination[:, None] == jnp.arange(expert_count * capacity, dtype=jnp.int32)[None, :]
    ).astype(jnp.float32)
    token_hot = (
        (jnp.arange(row_count * TOPK, dtype=jnp.int32) // TOPK)[:, None]
        == jnp.arange(row_count, dtype=jnp.int32)[None, :]
    ).astype(jnp.float32)
    placement = jnp.einsum("cx,ct->xt", dest_hot, token_hot, precision=HIGHEST).astype(jnp.bfloat16)
    outgoing = jnp.dot(placement, mixed, preferred_element_type=jnp.float32).astype(jnp.bfloat16)
    outgoing = outgoing.reshape(expert_count, capacity, model_width)
    combine_map = jnp.einsum(
        "ct,cx->tx", token_hot, dest_hot * gates_flat[:, None], precision=HIGHEST
    )
    w_gate_here = expert_w_gate[0]
    w_up_here = expert_w_up[0]
    w_down_here = expert_w_down[0]
    received = lax.all_to_all(outgoing, "req", split_axis=0, concat_axis=0, tiled=True)
    sources = received.shape[0]
    item_count = received.shape[1]
    flat_rows = received.reshape(sources * item_count, model_width)
    gate_pre = jnp.dot(flat_rows, w_gate_here, preferred_element_type=jnp.float32)
    up_pre = jnp.dot(flat_rows, w_up_here, preferred_element_type=jnp.float32)
    hidden = (jax.nn.silu(gate_pre) * up_pre).astype(jnp.bfloat16)
    partial_out = jnp.dot(hidden, w_down_here, preferred_element_type=jnp.float32).reshape(
        sources, item_count, model_width
    )
    summed = lax.psum(partial_out, "tp").astype(jnp.bfloat16)
    returned = lax.all_to_all(summed, "req", split_axis=0, concat_axis=0, tiled=True)
    returned_cols = returned.shape[2]
    moe_out = jnp.dot(
        combine_map,
        returned.reshape(expert_count * capacity, returned_cols).astype(jnp.float32),
        precision=HIGHEST,
    )
    moe_out = lax.dynamic_slice_in_dim(moe_out, tp_index * col_share, col_share, 1)
    mixed_cols = lax.dynamic_slice_in_dim(mixed, tp_index * col_share, col_share, 1)
    piece = lax.all_gather(mixed_cols, "req", axis=0, tiled=True)
    gate_part = jnp.dot(piece, shared_w_gate, preferred_element_type=jnp.float32)
    up_part = jnp.dot(piece, shared_w_up, preferred_element_type=jnp.float32)
    shared_pre = jnp.concatenate([gate_part, up_part], axis=1)
    shared_pre = lax.psum(shared_pre, "tp")
    unit_count = shared_w_gate.shape[1]
    shared_hidden = (jax.nn.silu(shared_pre[:, :unit_count]) * shared_pre[:, unit_count:]).astype(
        jnp.bfloat16
    )
    shared_mine = lax.psum_scatter(
        jnp.dot(shared_hidden, shared_w_down, preferred_element_type=jnp.float32),
        "req",
        scatter_dimension=0,
        tiled=True,
    )
    switch = jax.nn.sigmoid(jnp.dot(mixed, shared_switch, preferred_element_type=jnp.float32))
    resid_mine = lax.dynamic_slice_in_dim(resid, tp_index * col_share, col_share, 1)
    final = resid_mine + moe_out + switch[:, None] * shared_mine
    return final.astype(jnp.bfloat16).reshape(req_rows, step_count, col_share)


def solution(mesh):
    return jax.shard_map(
        per_device,
        mesh=mesh,
        in_specs=(
            P("req", None, None),
            P(),
            P(None, None, "tp"),
            P(None, "tp"),
            P("tp", None),
            P("req", None, "tp"),
            P("req", None, "tp"),
            P(),
            P(),
            P(),
            P("req", None, None),
            P("req", None, None),
            P("req", None, "tp"),
            P("req", None, "tp"),
            P("req", "tp", None),
            P("tp", "req"),
            P("tp", "req"),
            P("req", "tp"),
            P(),
        ),
        out_specs=P("req", None, "tp"),
        check_vma=False,
    )
```

profile of v0, /device:TPU:0, one launch (start us, length us, event | category | flops | bytes accessed | tf_op | source)
XLA Modules:
  0.0 321.9 jit_solution(12219065390824033137)
XLA Ops:
  10.9 1.4 gather_fusion
  12.4 3.8 %fusion.28 = f32[3,4,3,512]{3,1,2,0:T(4,128)S(1)} fusion(bf16[2048,3,512]{2,0,1:T(8,128)(2,1)} %param.21, bf16[3,4,2048]{2,1,0:T(4,128)(2,1)} %param.19, f32[2048]{0:T(1024)S(1)} %convert_element_type.78, f32[3,4]{1,0:T(4,128)S(1)} %add_rsqrt_fusion, f32[3,512]{1,0:T(4,128)S(1)} %convert_element_type.80), kind=kOutput, calls=%fused_computation.23 | convolution fusion | flops 75614208 | bytes 6428720 | tf_op jit(solution)/shard_map/rsd,dcf->rscf/dot_general | solution.py:74
  17.7 32.3 %all_gather.6 = bf16[24,4,4,128]{3,2,1,0:T(4,128)(2,1)S(1)} all-gather(bf16[3,4,4,128]{3,2,1,0:T(4,128)(2,1)S(1)} %copy.91), channel_id=1, replica_groups=mesh['req'=8,'tp'=4] {'req'}, dimensions={0}, use_global_device_ids=true | all-gather | bytes 110592 | tf_op jit(solution)/shard_map/all_gather | solution.py:83
  50.8 5.4 %fusion.114 = (f32[40,4,4]{1,2,0:T(4,128)S(1)}, f32[40,4,4,128]{3,1,2,0:T(4,128)S(1)}) fusion(bf16[40,4,4,128]{3,2,1,0:T(4,128)(2,1)S(1)} %gather_fusion.1, pred[40,128]{1,0:T(8,128)(4,1)S(1)} %fusion.81, bf16[40,128,512]{2,1,0:T(8,128)(2,1)} %param.24), kind=kOutput, calls=%fused_computation.150 | convolution fusion | flops 21216640 | bytes 5742080 | tf_op jit(solution)/shard_map/pshd,pkhd->pshk/dot_general | solution.py:97
  56.5 22.2 %pmax.7 = f32[24,4,4]{0,2,1:T(4,128)} all-reduce(f32[24,4,4]{0,2,1:T(4,128)S(1)} %select_reduce_fusion), channel_id=1, replica_groups=mesh['req'=8,'tp'=4] {'req'}, use_global_device_ids=true, to_apply=%region_6.7 | all-reduce | flops 384 | bytes 3072 | tf_op jit(solution)/shard_map/pmax | solution.py:118
  79.8 4.1 %fusion.15 = f32[40,4,4,128]{3,1,2,0:T(4,128)S(1)} fusion(f32[40,4,4,128]{3,1,2,0:T(4,128)S(1)} %get-tuple-element.28, f32[40,4,4]{1,2,0:T(4,128)S(1)} %get-tuple-element.27, pred[40,128]{1,0:T(8,128)(4,1)} %copy-done.7, bf16[40,128,512]{2,1,0:T(8,128)(2,1)} %param.25), kind=kOutput, calls=%fused_computation.17 | convolution fusion | flops 21217280 | bytes 5905920 | tf_op jit(solution)/shard_map/pshk,pkhd->pshd/dot_general | solution.py:105
  86.9 2.0 fusion.21
  92.2 17.4 %psum.36 = f32[24,4,4]{0,2,1:T(4,128)S(1)} all-reduce(f32[24,4,4]{0,2,1:T(4,128)S(1)} %bitcast.134), channel_id=1, replica_groups=mesh['req'=8,'tp'=4] {'req'}, use_global_device_ids=true, to_apply=%region_10.11 | all-reduce | flops 384 | bytes 3072 | tf_op jit(solution)/shard_map/psum | solution.py:120
  110.4 46.0 %all-reduce.7.cloned.1.call-done = f32[24,4,4,128]{3,0,2,1:T(8,128)} async-done(((f32[24,4,4,128]{3,0,2,1:T(8,128)}), f32[24,4,4,128]{3,0,2,1:T(8,128)}) %all-reduce.7.cloned.1.call-update) | async-done | bytes 196624 | tf_op jit(solution)/shard_map/psum | solution.py:120
  161.1 28.1 %all-reduce.9.cloned.1.call-done = f32[12,2048]{1,0:T(8,128)} async-done(((f32[12,2048]{1,0:T(8,128)}), f32[12,2048]{1,0:T(8,128)}) %all-reduce.9.cloned.1.call-update) | async-done | bytes 98320 | tf_op jit(solution)/shard_map/psum | solution.py:148
  190.4 30.6 %all-gather = bf16[8,12,512]{2,1,0:T(8,128)(2,1)S(1)} all-gather(bf16[1,12,512]{2,1,0:T(8,128)(2,1)S(1)} %dynamic-slice_bitcast_fusion), channel_id=1, replica_groups=mesh['req'=8,'tp'=4] {'req'}, dimensions={0}, use_global_device_ids=true | all-gather | bytes 110592 | tf_op jit(solution)/shard_map/all_gather | solution.py:196
  221.4 1.5 fusion.117
  224.9 5.5 %all-to-all-start = ((bf16[8,6,2048]{2,1,0:T(8,128)(2,1)}), bf16[8,6,2048]{2,1,0:T(8,128)(2,1)S(1)}, u32[]{:S(2)}, u32[]{:S(2)}) async-start(bf16[8,6,2048]{2,1,0:T(8,128)(2,1)} %reshape.235), calls=%async_computation | async-start | bytes 524288 | tf_op jit(solution)/shard_map/all_to_all | solution.py:176
  231.9 25.2 %all-reduce.11.cloned.1.call-done = f32[96,1408]{1,0:T(8,128)} async-done(((f32[96,1408]{1,0:T(8,128)}), f32[96,1408]{1,0:T(8,128)}) %all-reduce.11.cloned.1.call-update) | async-done | bytes 540688 | tf_op jit(solution)/shard_map/psum | solution.py:200
  257.1 1.6 fusion.56
  258.7 1.9 fusion.13
  260.7 1.9 fusion.25
  262.6 1.7 fusion.9
  264.3 14.5 %all-reduce.12 = bf16[8,6,2048]{2,0,1:T(8,128)(2,1)S(1)} all-reduce(f32[8,6,2048]{2,0,1:T(8,128)S(1)} %fusion.9), channel_id=1, replica_groups=mesh['req'=8,'tp'=4] {'tp'}, use_global_device_ids=true, to_apply=%region_16.17 | all-reduce | flops 98304 | bytes 589824 | tf_op jit(solution)/shard_map/psum | solution.py:186
  279.6 5.4 %all-to-all-start.1 = ((bf16[8,6,2048]{2,1,0:T(8,128)(2,1)}), bf16[8,6,2048]{2,1,0:T(8,128)(2,1)S(1)}, u32[]{:S(2)}, u32[]{:S(2)}) async-start(bf16[8,6,2048]{2,1,0:T(8,128)(2,1)} %copy.108), calls=%async_computation.1 | async-start | bytes 524288 | tf_op jit(solution)/shard_map/all_to_all | solution.py:187
  285.1 24.1 %fusion = f32[16,512]{1,0:T(8,128)S(1)} fusion(f32[96,512]{1,0:T(8,128)S(1)} %fusion.56), kind=kCustom, calls=%all-reduce-scatter | all-reduce-scatter fusion | flops 65537 | bytes 229888
  309.2 2.1 collective-permute-start
  311.2 1.3 collective-permute-start.1
  312.7 1.4 collective-permute-done.1
  (100 shorter events, 26.4 us)
Async XLA Ops:
  6.5 150.9 %copy-start = (bf16[512,2048]{1,0:T(8,128)(2,1)S(1)}, bf16[512,2048]{1,0:T(8,128)(2,1)}, u32[]{:S(2)}) copy-start(bf16[512,2048]{1,0:T(8,128)(2,1)} %param.23) | copy-start | bytes 6291460
  6.5 149.8 %all-reduce.7.cloned.1.call-start = ((), (), s32[]{:S(2)}) async-start(), calls=%async_computation.2 | async-start | bytes 393216 | tf_op jit(solution)/shard_map/psum | solution.py:120
  10.9 45.4 %copy-start.6 = (pred[24,40]{1,0:T(8,128)(4,1)}, pred[24,40]{1,0:T(8,128)(4,1)S(1)}, u32[]{:S(2)}) copy-start(pred[24,40]{1,0:T(8,128)(4,1)S(1)} %fusion.98) | copy-start | bytes 2884
  16.2 0.9 copy-start.5
  17.1 0.6 copy-start.4
  50.8 27.9 %copy-start.7 = (pred[40,128]{1,0:T(8,128)(4,1)}, pred[40,128]{1,0:T(8,128)(4,1)S(1)}, u32[]{:S(2)}) copy-start(pred[40,128]{1,0:T(8,128)(4,1)S(1)} %fusion.81) | copy-start | bytes 15364
  56.3 22.3 %copy-start.3 = (f32[40,4,4]{0,2,1:T(4,128)}, f32[40,4,4]{0,2,1:T(4,128)S(1)}, u32[]{:S(2)}) copy-start(f32[40,4,4]{0,2,1:T(4,128)S(1)} %copy.96) | copy-start | bytes 7684
  56.5 22.2 %copy-start.2 = (f32[24,4,4]{0,2,1:T(4,128)}, f32[24,4,4]{0,2,1:T(4,128)S(1)}, u32[]{:S(2)}) copy-start(f32[24,4,4]{0,2,1:T(4,128)S(1)} %select_reduce_fusion) | copy-start | bytes 4612
  79.8 141.2 %copy-start.1 = (bf16[512,704]{0,1:T(8,128)(2,1)S(1)}, bf16[512,704]{0,1:T(8,128)(2,1)}, u32[]{:S(2)}) copy-start(bf16[512,704]{0,1:T(8,128)(2,1)} %param.35) | copy-start | bytes 2162692
  86.8 143.8 %copy-start.8 = (bf16[2048]{0:T(1024)(128)(2,1)S(1)}, bf16[2048]{0:T(1024)(128)(2,1)}, u32[]{:S(2)}) copy-start(bf16[2048]{0:T(1024)(128)(2,1)} %param.37) | copy-start | bytes 12292
  86.8 143.8 %copy-start.9 = (u32[32]{0:T(128)S(1)}, u32[32]{0:T(128)}, u32[]{:S(2)}) copy-start(u32[32]{0:T(128)} %constant.87) | copy-start | bytes 388
  88.9 100.4 %all-reduce.9.cloned.1.call-start = ((), (), s32[]{:S(2)}) async-start(), calls=%async_computation.3 | async-start | bytes 262144 | tf_op jit(solution)/shard_map/psum | solution.py:148
  158.5 98.5 %all-reduce.11.cloned.1.call-start = ((), (), s32[]{:S(2)}) async-start(), calls=%async_computation.4 | async-start | bytes 1081344 | tf_op jit(solution)/shard_map/psum | solution.py:200
  224.9 33.8 %all-to-all-start = ((bf16[8,6,2048]{2,1,0:T(8,128)(2,1)}), bf16[8,6,2048]{2,1,0:T(8,128)(2,1)S(1)}, u32[]{:S(2)}, u32[]{:S(2)}) async-start(bf16[8,6,2048]{2,1,0:T(8,128)(2,1)} %reshape.235), calls=%async_computation | async-start | bytes 524288 | tf_op jit(solution)/shard_map/all_to_all | solution.py:176
  279.6 34.7 %all-to-all-start.1 = ((bf16[8,6,2048]{2,1,0:T(8,128)(2,1)}), bf16[8,6,2048]{2,1,0:T(8,128)(2,1)S(1)}, u32[]{:S(2)}, u32[]{:S(2)}) async-start(bf16[8,6,2048]{2,1,0:T(8,128)(2,1)} %copy.108), calls=%async_computation.1 | async-start | bytes 524288 | tf_op jit(solution)/shard_map/all_to_all | solution.py:187
  309.2 4.9 %collective-permute-start = (f32[16,512]{1,0:T(8,128)S(1)}, f32[16,512]{1,0:T(8,128)S(1)}, u32[]{:S(2)}, u32[]{:S(2)}) collective-permute-start(f32[16,512]{1,0:T(8,128)S(1)} %fusion), channel_id=1, source_target_pairs={{0,4},{4,8},{8,12},{12,16},{16,20},{20,24},{24,28},{1,5},{5,9},{9,... | collective-permute-start | bytes 98312
  311.2 2.9 collective-permute-start.1
Sparse Core Ops, SparseCore 0:
  89.0 67.3 all-reduce.6
  158.8 30.4 all-reduce.8
  224.0 33.0 all-reduce.10
where the time goes:
time: 323 us; the launch traced here: 322 us
  blocking collectives  141 us (44%)
  waiting for transfers between devices  101 us (31%)
  matrix products  29.5 us (9%)
  starting transfers between devices  14.3 us (4%)
  between operations  14.2 us (4%)
  local copies, waits for them, and re-layouts  11.4 us (4%)
  other arithmetic  10.7 us (3%)
    psum x1, waiting for transfers between devices, per_device(): lax.psum((local_out * rescale[..., None], local_sum * rescale), 'req')  46 us
    all_gather x1, blocking collectives, per_device(): query_all = lax.all_gather(query_new, 'req', axis=0, tiled=True)  32.3 us
    all_gather x1, blocking collectives, per_device(): piece = lax.all_gather(mixed_cols, 'req', axis=0, tiled=True)  30.6 us
    psum x1, waiting for transfers between devices, per_device(): attn_full = lax.psum(attn_part, 'tp')  28.1 us
    psum x1, waiting for transfers between devices, per_device(): shared_pre = lax.psum(shared_pre, 'tp')  25.2 us
    unnamed x1, blocking collectives  24.1 us
    pmax x1, blocking collectives, per_device(): global_max = lax.pmax(local_max, 'req')  22.2 us
    psum x1, blocking collectives, per_device(): lax.psum((local_out * rescale[..., None], local_sum * rescale), 'req')  17.4 us
  transfers between devices with their start and end apart: 7, of which 4 were waited for; matrix products, arithmetic and copies ran while one was open for 11% of the time, Pallas kernels for 0%

commit v1 on v0

--- a/solution.py
+++ b/solution.py
@@ -10,6 +10,7 @@
 EPS = 1e-06
 THETA = 1000000.0
 HIGHEST = lax.Precision.HIGHEST
+list_meshes = lambda t0, peer_axis: jnp.sum(jax.lax.all_gather(t0, peer_axis), 0)
 
 
 def rms_norm(inputs, gain_vector):
@@ -197,7 +198,7 @@
     gate_part = jnp.dot(piece, shared_w_gate, preferred_element_type=jnp.float32)
     up_part = jnp.dot(piece, shared_w_up, preferred_element_type=jnp.float32)
     shared_pre = jnp.concatenate([gate_part, up_part], axis=1)
-    shared_pre = lax.psum(shared_pre, "tp")
+    shared_pre = list_meshes(shared_pre, "tp")
     unit_count = shared_w_gate.shape[1]
     shared_hidden = (jax.nn.silu(shared_pre[:, :unit_count]) * shared_pre[:, unit_count:]).astype(
         jnp.bfloat16

time: 323 us -> 307 us (0.950)
  waiting for transfers between devices: 101 us -> 95 us
  local copies, waits for them, and re-layouts: 11.4 us -> 7.73 us
    psum x1 -> x0, waiting for transfers between devices: 25.2 us -> none  [per_device(): shared_pre = lax.psum(shared_pre, 'tp')]
    all_to_all x1, waiting for transfers between devices: 0.01 us -> 7.76 us  [per_device(): lax.all_to_all(summed, 'req', split_axis=0, concat_axis=0, tiled=True)]
    all_to_all x1, waiting for transfers between devices: 0.01 us -> 6.85 us  [per_device(): lax.all_to_all(outgoing, 'req', split_axis=0, concat_axis=0, tiled=True)]
  transfers between devices with their start and end apart: 7 -> 7, of which waited for: 4 -> 5; matrix products, arithmetic and copies ran while one was open for 11% -> 4% of each run, Pallas kernels for 0% -> 0%
where the time goes in v1:
time: 307 us; the launch traced here: 306 us
  blocking collectives  139 us (45%)
  waiting for transfers between devices  95 us (31%)
  matrix products  26.7 us (9%)
  between operations  14.2 us (5%)
  starting transfers between devices  12.3 us (4%)
  other arithmetic  10.6 us (3%)
  local copies, waits for them, and re-layouts  7.73 us (3%)
    psum x1, waiting for transfers between devices, per_device(): lax.psum((local_out * rescale[..., None], local_sum * rescale), 'req')  49 us
    all_gather x1, blocking collectives, per_device(): query_all = lax.all_gather(query_new, 'req', axis=0, tiled=True)  32.3 us
    all_gather x1, blocking collectives, per_device(): piece = lax.all_gather(mixed_cols, 'req', axis=0, tiled=True)  30.6 us
    psum x1, waiting for transfers between devices, per_device(): attn_full = lax.psum(attn_part, 'tp')  30 us
    unnamed x1, blocking collectives  22.6 us
    pmax x1, blocking collectives, per_device(): global_max = lax.pmax(local_max, 'req')  21.6 us
    psum x1, blocking collectives, per_device(): lax.psum((local_out * rescale[..., None], local_sum * rescale), 'req')  17.6 us
    psum x1, blocking collectives, per_device(): summed = lax.psum(partial_out, 'tp').astype(jnp.bfloat16)  14.5 us
  transfers between devices with their start and end apart: 7, of which 5 were waited for; matrix products, arithmetic and copies ran while one was open for 4% of the time, Pallas kernels for 0%

profile of v1, /device:TPU:0, one launch (start us, length us, event | category | flops | bytes accessed | tf_op | source)
XLA Modules:
  0.0 305.8 jit_solution(15455347939930904715)
XLA Ops:
  10.9 1.4 gather_fusion
  12.3 3.8 %fusion.28 = f32[3,4,3,512]{3,1,2,0:T(4,128)S(1)} fusion(bf16[2048,3,512]{2,0,1:T(8,128)(2,1)} %param.21, bf16[3,4,2048]{2,1,0:T(4,128)(2,1)} %param.19, f32[2048]{0:T(1024)S(1)} %convert_element_type.78, f32[3,4]{1,0:T(4,128)S(1)} %add_rsqrt_fusion, f32[3,512]{1,0:T(4,128)S(1)} %convert_element_type.80), kind=kOutput, calls=%fused_computation.23 | convolution fusion | flops 75614208 | bytes 6428720 | tf_op jit(solution)/shard_map/rsd,dcf->rscf/dot_general | solution.py:75
  16.5 32.3 %all_gather.12 = bf16[24,4,4,128]{3,2,1,0:T(4,128)(2,1)S(1)} all-gather(bf16[3,4,4,128]{3,2,1,0:T(4,128)(2,1)S(1)} %copy.91), channel_id=1, replica_groups=mesh['req'=8,'tp'=4] {'req'}, dimensions={0}, use_global_device_ids=true | all-gather | bytes 110592 | tf_op jit(solution)/shard_map/all_gather | solution.py:84
  49.6 5.4 %fusion.114 = (f32[40,4,4]{1,2,0:T(4,128)S(1)}, f32[40,4,4,128]{3,1,2,0:T(4,128)S(1)}) fusion(bf16[40,4,4,128]{3,2,1,0:T(4,128)(2,1)S(1)} %gather_fusion.1, pred[40,128]{1,0:T(8,128)(4,1)S(1)} %fusion.81, bf16[40,128,512]{2,1,0:T(8,128)(2,1)} %param.24), kind=kOutput, calls=%fused_computation.150 | convolution fusion | flops 21216640 | bytes 5742080 | tf_op jit(solution)/shard_map/pshd,pkhd->pshk/dot_general | solution.py:98
  55.3 21.6 %pmax.7 = f32[24,4,4]{0,2,1:T(4,128)S(1)} all-reduce(f32[24,4,4]{0,2,1:T(4,128)S(1)} %select_reduce_fusion), channel_id=1, replica_groups=mesh['req'=8,'tp'=4] {'req'}, use_global_device_ids=true, to_apply=%region_6.7 | all-reduce | flops 384 | bytes 3072 | tf_op jit(solution)/shard_map/pmax | solution.py:119
  77.5 4.2 %fusion.15 = f32[40,4,4,128]{3,1,2,0:T(4,128)S(1)} fusion(f32[40,4,4,128]{3,1,2,0:T(4,128)} %copy-done.2, f32[40,4,4]{1,2,0:T(4,128)S(1)} %get-tuple-element.27, pred[40,128]{1,0:T(8,128)(4,1)S(1)} %fusion.81, bf16[40,128,512]{2,1,0:T(8,128)(2,1)} %param.25), kind=kOutput, calls=%fused_computation.17 | convolution fusion | flops 21217280 | bytes 5905920 | tf_op jit(solution)/shard_map/pshk,pkhd->pshd/dot_general | solution.py:106
  84.3 17.6 %psum.29 = f32[24,4,4]{0,2,1:T(4,128)S(1)} all-reduce(f32[24,4,4]{0,2,1:T(4,128)S(1)} %bitcast.136), channel_id=1, replica_groups=mesh['req'=8,'tp'=4] {'req'}, use_global_device_ids=true, to_apply=%region_10.11 | all-reduce | flops 384 | bytes 3072 | tf_op jit(solution)/shard_map/psum | solution.py:121
  102.0 49.0 %all-reduce.6.cloned.1.call-done = f32[24,4,4,128]{3,0,2,1:T(8,128)} async-done(((f32[24,4,4,128]{3,0,2,1:T(8,128)}), f32[24,4,4,128]{3,0,2,1:T(8,128)}) %all-reduce.6.cloned.1.call-update) | async-done | bytes 196624 | tf_op jit(solution)/shard_map/psum | solution.py:121
  154.0 30.0 %all-reduce.8.cloned.1.call-done = f32[12,2048]{1,0:T(8,128)} async-done(((f32[12,2048]{1,0:T(8,128)}), f32[12,2048]{1,0:T(8,128)}) %all-reduce.8.cloned.1.call-update) | async-done | bytes 98320 | tf_op jit(solution)/shard_map/psum | solution.py:149
  185.1 30.6 %all-gather.1 = bf16[8,12,512]{2,1,0:T(8,128)(2,1)S(1)} all-gather(bf16[1,12,512]{2,1,0:T(8,128)(2,1)S(1)} %dynamic-slice_bitcast_fusion), channel_id=1, replica_groups=mesh['req'=8,'tp'=4] {'req'}, dimensions={0}, use_global_device_ids=true | all-gather | bytes 110592 | tf_op jit(solution)/shard_map/all_gather | solution.py:197
  216.1 1.5 fusion.117
  220.2 5.5 %all-to-all-start = ((bf16[8,6,2048]{2,1,0:T(8,128)(2,1)}), bf16[8,6,2048]{2,1,0:T(8,128)(2,1)S(1)}, u32[]{:S(2)}, u32[]{:S(2)}) async-start(bf16[8,6,2048]{2,1,0:T(8,128)(2,1)} %reshape.235), calls=%async_computation | async-start | bytes 524288 | tf_op jit(solution)/shard_map/all_to_all | solution.py:177
  227.1 6.8 %all-to-all-done = bf16[8,6,2048]{2,1,0:T(8,128)(2,1)S(1)} async-done(((bf16[8,6,2048]{2,1,0:T(8,128)(2,1)}), bf16[8,6,2048]{2,1,0:T(8,128)(2,1)S(1)}, u32[]{:S(2)}, u32[]{:S(2)}) %all-to-all-start) | async-done | bytes 196640 | tf_op jit(solution)/shard_map/all_to_all | solution.py:177
  234.0 1.9 fusion.13
  235.9 1.9 fusion.25
  237.9 1.7 fusion.9
  239.6 14.5 %all-reduce.9 = bf16[8,6,2048]{2,0,1:T(8,128)(2,1)S(1)} all-reduce(f32[8,6,2048]{2,0,1:T(8,128)S(1)} %fusion.9), channel_id=1, replica_groups=mesh['req'=8,'tp'=4] {'tp'}, use_global_device_ids=true, to_apply=%region_16.17 | all-reduce | flops 98304 | bytes 589824 | tf_op jit(solution)/shard_map/psum | solution.py:187
  254.9 3.4 %all-to-all-start.1 = ((bf16[8,6,2048]{2,1,0:T(8,128)(2,1)}), bf16[8,6,2048]{2,1,0:T(8,128)(2,1)S(1)}, u32[]{:S(2)}, u32[]{:S(2)}) async-start(bf16[8,6,2048]{2,1,0:T(8,128)(2,1)} %copy.108), calls=%async_computation.1 | async-start | bytes 524288 | tf_op jit(solution)/shard_map/all_to_all | solution.py:188
  258.7 7.8 %all-to-all-done.1 = bf16[8,6,2048]{2,1,0:T(8,128)(2,1)S(1)} async-done(((bf16[8,6,2048]{2,1,0:T(8,128)(2,1)}), bf16[8,6,2048]{2,1,0:T(8,128)(2,1)S(1)}, u32[]{:S(2)}, u32[]{:S(2)}) %all-to-all-start.1) | async-done | bytes 196640 | tf_op jit(solution)/shard_map/all_to_all | solution.py:188
  266.6 2.6 reduce_sum.92
  269.2 1.6 fusion.56
  270.7 22.6 %fusion = f32[16,512]{1,0:T(8,128)S(1)} fusion(f32[96,512]{1,0:T(8,128)S(1)} %fusion.56), kind=kCustom, calls=%all-reduce-scatter | all-reduce-scatter fusion | flops 65537 | bytes 229888
  293.4 2.1 collective-permute-start
  297.0 1.4 collective-permute-done.1
  (97 shorter events, 20.5 us)
Async XLA Ops:
  6.5 145.6 %copy-start = (bf16[512,2048]{1,0:T(8,128)(2,1)S(1)}, bf16[512,2048]{1,0:T(8,128)(2,1)}, u32[]{:S(2)}) copy-start(bf16[512,2048]{1,0:T(8,128)(2,1)} %param.23) | copy-start | bytes 6291460
  6.5 144.5 %all-reduce.6.cloned.1.call-start = ((), (), s32[]{:S(2)}) async-start(), calls=%async_computation.2 | async-start | bytes 393216 | tf_op jit(solution)/shard_map/psum | solution.py:121
  55.0 21.9 %copy-start.2 = (f32[40,4,4,128]{3,1,2,0:T(4,128)}, f32[40,4,4,128]{3,1,2,0:T(4,128)S(1)}, u32[]{:S(2)}) copy-start(f32[40,4,4,128]{3,1,2,0:T(4,128)S(1)} %get-tuple-element.28) | copy-start | bytes 983044
  77.4 75.8 %copy-start.3 = (bf16[3,4,2048]{2,1,0:T(4,128)(2,1)S(1)}, bf16[3,4,2048]{2,1,0:T(4,128)(2,1)}, u32[]{:S(2)}) copy-start(bf16[3,4,2048]{2,1,0:T(4,128)(2,1)} %param.19) | copy-start | bytes 147460
  77.4 138.3 %copy-start.1 = (bf16[512,704]{0,1:T(8,128)(2,1)S(1)}, bf16[512,704]{0,1:T(8,128)(2,1)}, u32[]{:S(2)}) copy-start(bf16[512,704]{0,1:T(8,128)(2,1)} %param.35) | copy-start | bytes 2162692
  81.6 136.9 %copy-start.4 = (s32[3,4,4]{2,1,0:T(4,128)S(1)}, s32[3,4,4]{2,1,0:T(4,128)}, u32[]{:S(2)}) copy-start(s32[3,4,4]{2,1,0:T(4,128)} %param.29) | copy-start | bytes 580
  82.3 143.4 %copy-start.5 = (f32[3,4,4]{2,1,0:T(4,128)S(1)}, f32[3,4,4]{2,1,0:T(4,128)}, u32[]{:S(2)}) copy-start(f32[3,4,4]{2,1,0:T(4,128)} %param.30) | copy-start | bytes 580
  82.3 143.5 %copy-start.6 = (bf16[2048]{0:T(1024)(128)(2,1)S(1)}, bf16[2048]{0:T(1024)(128)(2,1)}, u32[]{:S(2)}) copy-start(bf16[2048]{0:T(1024)(128)(2,1)} %param.37) | copy-start | bytes 12292
  82.3 143.5 %copy-start.7 = (u32[32]{0:T(128)S(1)}, u32[32]{0:T(128)}, u32[]{:S(2)}) copy-start(u32[32]{0:T(128)} %constant.87) | copy-start | bytes 388
  83.6 100.4 %all-reduce.8.cloned.1.call-start = ((), (), s32[]{:S(2)}) async-start(), calls=%async_computation.3 | async-start | bytes 262144 | tf_op jit(solution)/shard_map/psum | solution.py:149
  153.2 113.4 %all-gather.4.cloned.1.call-start = ((), (), s32[]{:S(2)}) async-start(), calls=%async_computation.4 | async-start | bytes 2703360 | tf_op jit(solution)/shard_map/all_gather | solution.py:13
  220.2 13.7 %all-to-all-start = ((bf16[8,6,2048]{2,1,0:T(8,128)(2,1)}), bf16[8,6,2048]{2,1,0:T(8,128)(2,1)S(1)}, u32[]{:S(2)}, u32[]{:S(2)}) async-start(bf16[8,6,2048]{2,1,0:T(8,128)(2,1)} %reshape.235), calls=%async_computation | async-start | bytes 524288 | tf_op jit(solution)/shard_map/all_to_all | solution.py:177
  254.9 11.6 %all-to-all-start.1 = ((bf16[8,6,2048]{2,1,0:T(8,128)(2,1)}), bf16[8,6,2048]{2,1,0:T(8,128)(2,1)S(1)}, u32[]{:S(2)}, u32[]{:S(2)}) async-start(bf16[8,6,2048]{2,1,0:T(8,128)(2,1)} %copy.108), calls=%async_computation.1 | async-start | bytes 524288 | tf_op jit(solution)/shard_map/all_to_all | solution.py:188
  293.4 5.0 %collective-permute-start = (f32[16,512]{1,0:T(8,128)S(1)}, f32[16,512]{1,0:T(8,128)S(1)}, u32[]{:S(2)}, u32[]{:S(2)}) collective-permute-start(f32[16,512]{1,0:T(8,128)S(1)} %fusion), channel_id=1, source_target_pairs={{0,4},{4,8},{8,12},{12,16},{16,20},{20,24},{24,28},{1,5},{5,9},{9,... | collective-permute-start | bytes 98312
  295.5 2.9 collective-permute-start.1
Sparse Core Ops, SparseCore 0:
  83.7 67.3 all-reduce.5
  153.5 30.4 all-reduce.7
  218.7 22.9 all-gather.3
